TPU v7x, 256 devices: a whole 4x4x8 slice. The times are simulated.
256 devices in a mesh: lat: 8 (over y, z_lo), lon: 8 (over x, core), dp: 4 (over z_hi).
Axes of the slice: x: 4, y: 4, z: 8 (z_hi: 4, z_lo: 2; z = z_hi * 2 + z_lo), core: 2. Of those that a mesh axis runs over, the one named last changes fastest.
Arguments:
- state_grid: bfloat16 [4, 384, 768, 128], P('dp', ('lat', 'lon')), may hold values from -6 to 6
- cotangent: bfloat16 [4, 384, 768, 128], P('dp', ('lat', 'lon')), may hold values from -6 to 6
- legendre: bfloat16 [384, 384, 384], P(('lat', 'lon')), may hold values from -0.3125 to 0.3125
- wave_ids: int32 [384], replicated, may hold values from 0 to 383, each once
- weights: bfloat16 [384, 2, 4, 1024], P('lat'), may hold values from -0.75 to 0.75
Outputs:
- input_grad: bfloat16 [4, 384, 768, 128], P('dp', ('lat', 'lon'))
- weight_grad: float32 [384, 2, 4, 1024], P('lat')
Inputs may be any that keep to these rules, and one draw needn't show every extreme that they name: wave_ids[j] is the wavenumber of slot j; each of 0 to 383 stands in exactly one slot.
All inputs are finite; a program needn't handle non-finite values.
Results may differ from a plain program's by a relative error of at most 0.034.
Values may be sent and summed in bfloat16 or wider, within the bound.
No kernel may reach another device: no remote copies, remote signals or barrier semaphores. Data moves between devices by JAX's collectives and lax.ppermute only.
A program may use at most 128 MiB of HBM per device.

v0:
```python
import math

import jax
import jax.numpy as jnp
from jax import lax
from jax.sharding import PartitionSpec as P

NLON = 768
GROUPS = 4
GROUP_WIDTH = 32


def build_tables(wave_ids):
    columns = jnp.arange(NLON, dtype=jnp.int32)
    phase_int = wave_ids[:, None] * columns[None, :] % NLON
    angles = phase_int.astype(jnp.float32) * jnp.float32(2.0 * math.pi / NLON)
    factor = jnp.float32(1.0 / math.sqrt(NLON))
    paired = jnp.stack([jnp.cos(angles) * factor, -jnp.sin(angles) * factor], axis=1)
    forward_table = paired.reshape(2 * wave_ids.shape[0], NLON)
    doubling = jnp.where(wave_ids == 0, 1.0, 2.0).astype(jnp.float32)
    inverse_table = forward_table * jnp.repeat(doubling, 2)[:, None]
    return (forward_table.astype(jnp.bfloat16), inverse_table.astype(jnp.bfloat16))


def build_kernel(weights):
    degree_count = weights.shape[0]
    real_part = weights[:, 0].reshape(degree_count, GROUPS, GROUP_WIDTH, GROUP_WIDTH)
    imag_part = weights[:, 1].reshape(degree_count, GROUPS, GROUP_WIDTH, GROUP_WIDTH)
    upper_rows = jnp.stack([real_part, imag_part], axis=3)
    lower_rows = jnp.stack([-imag_part, real_part], axis=3)
    return jnp.stack([upper_rows, lower_rows], axis=2)


def gelu_slope(branch):
    normal_cdf = 0.5 * (1.0 + lax.erf(branch * (1.0 / math.sqrt(2.0))))
    density = jnp.exp(-0.5 * branch * branch) * (1.0 / math.sqrt(2.0 * math.pi))
    return normal_cdf + branch * density


def shards(state_grid, cotangent, legendre, wave_ids, weights):
    lat_count = lax.axis_size("lat")
    lon_count = lax.axis_size("lon")
    samples, rows_dev, lon_cells, channels = state_grid.shape
    slot_count, lat_cells, degree_count = legendre.shape
    slot_reals = 2 * slot_count
    first_slot = (lax.axis_index("lat") * lon_count + lax.axis_index("lon")) * slot_count
    held_waves = lax.dynamic_slice_in_dim(wave_ids, first_slot, slot_count)
    degree_ids = jnp.arange(degree_count, dtype=jnp.int32)
    masked = jnp.where(
        degree_ids[None, None, :] >= held_waves[:, None, None],
        legendre,
        jnp.zeros((), legendre.dtype),
    )
    slot_order = wave_ids.reshape(lat_count, lon_count, slot_count).transpose(1, 0, 2).reshape(-1)
    forward_table, inverse_table = build_tables(slot_order)
    kernel = build_kernel(weights)

    def analyze(source, twiddle):
        spectra = jnp.einsum(
            "srnc,kn->srkc", source, twiddle, preferred_element_type=jnp.float32
        ).astype(jnp.bfloat16)
        gathered = lax.all_to_all(
            lax.all_to_all(spectra, "lon", split_axis=2, concat_axis=1, tiled=True),
            "lat",
            split_axis=2,
            concat_axis=1,
            tiled=True,
        )
        blocks = gathered.reshape(samples, lat_cells, slot_count, 2 * channels)
        spectral = jnp.einsum("samc,mal->slmc", blocks, masked, preferred_element_type=jnp.float32)
        spectral = spectral.astype(jnp.bfloat16).reshape(
            samples, degree_count, slot_reals, channels
        )
        return lax.all_to_all(spectral, "lat", split_axis=1, concat_axis=2, tiled=True)

    def synthesize(spectral, twiddle):
        joined = lax.all_to_all(spectral, "lat", split_axis=2, concat_axis=1, tiled=True)
        blocks = joined.reshape(samples, degree_count, slot_count, 2 * channels)
        spectra = jnp.einsum(
            "slmc,mal->samc", blocks, masked, preferred_element_type=jnp.float32
        ).astype(jnp.bfloat16)
        spectra = spectra.reshape(samples, lat_cells, slot_reals, channels)
        pencil = lax.all_to_all(
            lax.all_to_all(spectra, "lat", split_axis=1, concat_axis=2, tiled=True),
            "lon",
            split_axis=1,
            concat_axis=2,
            tiled=True,
        )
        return jnp.einsum("srkc,kn->srnc", pencil, twiddle, preferred_element_type=jnp.float32)

    def split_groups(spectral):
        return spectral.reshape(samples, spectral.shape[1], -1, 2, GROUPS, GROUP_WIDTH)

    coef_fwd = analyze(state_grid, forward_table)
    coef_six = split_groups(coef_fwd)
    mixed_coef = jnp.einsum(
        "slmpgi,lgpiqo->slmqgo", coef_six, kernel, preferred_element_type=jnp.float32
    ).astype(jnp.bfloat16)
    branch = synthesize(mixed_coef.reshape(coef_fwd.shape), inverse_table)
    pulled = (cotangent.astype(jnp.float32) * gelu_slope(branch)).astype(jnp.bfloat16)
    back_coef = analyze(pulled, inverse_table)
    back_six = split_groups(back_coef)
    outer_sums = jnp.einsum(
        "slmpgi,slmqgo->lgpiqo", coef_six, back_six, preferred_element_type=jnp.float32
    )
    real_grad = outer_sums[:, :, 0, :, 0, :] + outer_sums[:, :, 1, :, 1, :]
    imag_grad = outer_sums[:, :, 0, :, 1, :] - outer_sums[:, :, 1, :, 0, :]
    local_grad = jnp.stack([real_grad, imag_grad], axis=1).reshape(weights.shape)
    weight_grad = lax.psum(local_grad.astype(jnp.bfloat16), ("lon", "dp")).astype(jnp.float32)
    demixed = jnp.einsum(
        "slmqgo,lgpiqo->slmpgi", back_six, kernel, preferred_element_type=jnp.float32
    ).astype(jnp.bfloat16)
    returned = synthesize(demixed.reshape(back_coef.shape), forward_table)
    input_grad = (cotangent.astype(jnp.float32) + returned).astype(jnp.bfloat16)
    return (input_grad, weight_grad)


def solution(mesh):
    return jax.shard_map(
        shards,
        mesh=mesh,
        in_specs=(
            P("dp", ("lat", "lon"), None, None),
            P("dp", ("lat", "lon"), None, None),
            P(("lat", "lon"), None, None),
            P(),
            P("lat", None, None, None),
        ),
        out_specs=(P("dp", ("lat", "lon"), None, None), P("lat", None, None, None)),
        check_vma=False,
    )
```

profile of v0, /device:TPU:1, one launch (start us, length us, event | category | flops | bytes accessed | tf_op | source)
XLA Modules:
  0.0 724.8 jit_solution(13457028617643623277)
XLA Ops:
  8.2 4.9 cosine_multiply_fusion
  13.3 2.2 copy.215
  15.6 3.7 reshape.366
  19.3 2.4 fusion.14
  22.5 26.4 %all_to_all.192 = bf16[1,6,768,128]{3,1,0,2:T(8,128)(2,1)S(1)} all-to-all(bf16[1,6,768,128]{3,1,0,2:T(8,128)(2,1)S(1)} %copy.223), channel_id=1, replica_groups=mesh['lat'=8,'lon'=8,'dp'=4] {'lon'}, dimensions={2} | all-to-all | bytes 2359296 | tf_op jit(solution)/shard_map/all_to_all | solution.py:63
  49.2 1.5 copy.226
  50.7 5.7 all-to-all-start.1
  57.2 14.6 %all-to-all-done.1 = bf16[1,48,96,128]{3,1,0,2:T(8,128)(2,1)S(1)} async-done(((bf16[1,48,96,128]{3,1,0,2:T(8,128)(2,1)}), bf16[1,48,96,128]{3,1,0,2:T(8,128)(2,1)S(1)}, u32[]{:S(2)}, u32[]{:S(2)}) %all-to-all-start.1) | async-done | bytes 1179680 | tf_op jit(solution)/shard_map/all_to_all | solution.py:62
  71.8 3.0 copy.280
  74.8 4.4 reshape.378
  79.2 3.4 convolution_convert_fusion.1
  82.6 2.9 copy.229
  85.5 4.5 all-to-all-start.2
  91.2 1.6 copy.298
  94.0 2.2 copy.299
  96.2 2.7 maximum_bitcast_fusion
  98.9 3.0 pad_maximum_fusion
  101.9 12.7 %copy.232 = bf16[48,4,2,32,2,32]{3,5,2,4,1,0:T(8,128)(2,1)} copy(bf16[48,4,2,32,2,32]{0,5,4,3,1,2:T(8,128)(2,1)} %pad_maximum_fusion) | data formatting | bytes 3145728 | tf_op jit(solution)/shard_map/stack | solution.py:31
  114.6 1.7 copy.230
  116.3 2.7 copy.231
  119.0 8.3 %copy.270 = bf16[48,48,2,4,32,1]{1,4,2,5,3,0:T(8,128)(2,1)} copy(bf16[48,48,2,4,32,1]{0,4,3,2,1,5:T(8,128)(2,1)} %bitcast.179) | data formatting | bytes 2359296 | tf_op jit(solution)/shard_map/reshape.8
  127.3 6.7 fusion
  134.0 8.3 %copy.234 = bf16[1,48,48,2,4,32]{1,5,4,3,2,0:T(8,128)(2,1)} copy(bf16[1,48,48,2,4,32]{2,5,3,4,1,0:T(8,128)(2,1)} %fusion) | data formatting | bytes 2359296 | tf_op jit(solution)/shard_map/convert_element_type | solution.py:99
  142.3 3.2 copy.235
  145.4 19.3 %all_to_all.193 = bf16[1,48,96,128]{3,1,0,2:T(8,128)(2,1)} all-to-all(bf16[1,48,96,128]{3,1,0,2:T(8,128)(2,1)S(1)} %copy.235), channel_id=1, replica_groups=mesh['lat'=8,'lon'=8,'dp'=4] {'lat'}, dimensions={2} | all-to-all | bytes 2359296 | tf_op jit(solution)/shard_map/all_to_all | solution.py:77
  164.8 4.2 copy.283
  169.0 4.4 reshape.379
  173.4 3.5 convolution_convert_fusion.3
  176.9 2.9 copy.238
  179.8 20.7 %all_to_all.194 = bf16[1,384,12,128]{3,2,0,1:T(8,128)(2,1)S(1)} all-to-all(bf16[1,384,12,128]{3,2,0,1:T(8,128)(2,1)} %copy.238), channel_id=1, replica_groups=mesh['lat'=8,'lon'=8,'dp'=4] {'lat'}, dimensions={1} | all-to-all | bytes 2359296 | tf_op jit(solution)/shard_map/all_to_all | solution.py:84
  202.2 9.2 %all-to-all-start.5 = ((bf16[1,48,96,128]{3,2,0,1:T(8,128)(2,1)}), bf16[1,48,96,128]{3,2,0,1:T(8,128)(2,1)}, u32[]{:S(2)}, u32[]{:S(2)}) async-start(bf16[1,48,96,128]{3,2,0,1:T(8,128)(2,1)} %copy.241), calls=%async_computation.5 | async-start | bytes 2359296 | tf_op jit(solution)/shard_map/all_to_all | solution.py:83
  213.8 14.2 %all-to-all-done.5 = bf16[1,48,96,128]{3,2,0,1:T(8,128)(2,1)} async-done(((bf16[1,48,96,128]{3,2,0,1:T(8,128)(2,1)}), bf16[1,48,96,128]{3,2,0,1:T(8,128)(2,1)}, u32[]{:S(2)}, u32[]{:S(2)}) %all-to-all-start.5) | async-done | bytes 1179680 | tf_op jit(solution)/shard_map/all_to_all | solution.py:83
  229.4 4.8 fusion.15
  234.2 2.1 copy.244
  236.3 24.1 %all_to_all.195 = bf16[1,6,768,128]{3,1,0,2:T(8,128)(2,1)S(1)} all-to-all(bf16[1,6,768,128]{3,1,0,2:T(8,128)(2,1)S(1)} %copy.244), channel_id=1, replica_groups=mesh['lat'=8,'lon'=8,'dp'=4] {'lon'}, dimensions={2} | all-to-all | bytes 2359296 | tf_op jit(solution)/shard_map/all_to_all | solution.py:63
  261.1 18.7 %all_to_all.196 = bf16[1,48,96,128]{3,1,0,2:T(8,128)(2,1)S(1)} all-to-all(bf16[1,48,96,128]{3,1,0,2:T(8,128)(2,1)S(1)} %copy.247), channel_id=1, replica_groups=mesh['lat'=8,'lon'=8,'dp'=4] {'lat'}, dimensions={2} | all-to-all | bytes 2359296 | tf_op jit(solution)/shard_map/all_to_all | solution.py:62
  279.8 3.0 copy.284
  282.7 4.4 reshape.380
  287.2 2.4 convolution_convert_fusion
  289.5 2.0 copy.250
  291.5 3.6 all-to-all-start.8
  295.1 11.6 %copy.253 = bf16[48,4,2,32,2,32]{5,3,4,2,1,0:T(8,128)(2,1)} copy(bf16[48,4,2,32,2,32]{0,5,4,3,1,2:T(8,128)(2,1)} %pad_maximum_fusion) | data formatting | bytes 3145728 | tf_op jit(solution)/shard_map/stack | solution.py:31
  306.7 7.3 %all-to-all-done.8 = bf16[1,384,12,128]{3,2,0,1:T(8,128)(2,1)S(1)} async-done(((bf16[1,384,12,128]{3,2,0,1:T(8,128)(2,1)}), bf16[1,384,12,128]{3,2,0,1:T(8,128)(2,1)S(1)}, u32[]{:S(2)}, u32[]{:S(2)}) %all-to-all-start.8) | async-done | bytes 1179680 | tf_op jit(solution)/shard_map/all_to_all | solution.py:74
  314.3 2.7 copy.252
  317.0 8.3 %copy.273 = bf16[48,48,2,4,32,1]{1,4,2,5,3,0:T(8,128)(2,1)} copy(bf16[48,48,2,4,32,1]{0,4,3,2,1,5:T(8,128)(2,1)} %bitcast.182) | data formatting | bytes 2359296 | tf_op jit(solution)/shard_map/reshape.39
  325.3 6.8 fusion.1
  332.1 8.3 %copy.255 = bf16[1,48,48,2,4,32]{1,5,4,3,2,0:T(8,128)(2,1)} copy(bf16[1,48,48,2,4,32]{2,5,3,4,1,0:T(8,128)(2,1)} %fusion.1) | data formatting | bytes 2359296 | tf_op jit(solution)/shard_map/convert_element_type | solution.py:113
  340.4 3.2 copy.256
  343.5 20.2 %all_to_all.197 = bf16[1,48,96,128]{3,1,0,2:T(8,128)(2,1)S(1)} all-to-all(bf16[1,48,96,128]{3,1,0,2:T(8,128)(2,1)S(1)} %copy.256), channel_id=1, replica_groups=mesh['lat'=8,'lon'=8,'dp'=4] {'lat'}, dimensions={2} | all-to-all | bytes 2359296 | tf_op jit(solution)/shard_map/all_to_all | solution.py:77
  363.7 3.0 copy.287
  366.7 4.4 reshape.381
  371.1 2.4 convolution_convert_fusion.2
  373.5 2.0 copy.259
  375.5 3.8 all-to-all-start.10
  379.3 8.3 %copy.276 = bf16[48,48,2,4,32,1]{1,4,5,2,3,0:T(8,128)(2,1)} copy(bf16[48,48,2,4,32,1]{0,4,3,2,1,5:T(8,128)(2,1)} %bitcast.180) | data formatting | bytes 2359296 | tf_op jit(solution)/shard_map/reshape.8
  387.6 12.5 %fusion.41 = f32[48,4,2,32,2,32]{5,3,4,2,1,0:T(8,128)} fusion(bf16[48,48,2,4,32,1]{1,4,5,2,3,0:T(8,128)(2,1)} %copy.276, bf16[48,48,2,4,32,1]{1,4,2,5,3,0:T(8,128)(2,1)} %copy.273), kind=kOutput, calls=%fused_computation.66 | convolution fusion | flops 75497472 | bytes 5505024 | tf_op jit(solution)/shard_map/slmpgi,slmqgo->lgpiqo/dot_general | solution.py:104
  401.8 6.6 all-to-all-start.11
  408.4 7.5 %fusion.3 = (bf16[48,4,1,32,1,32]{5,3,4,2,1,0:T(8,128)(2,1)}, bf16[48,4,1,32,1,32]{5,3,4,2,1,0:T(8,128)(2,1)S(1)}) fusion(f32[48,4,2,32,2,32]{5,3,4,2,1,0:T(8,128)} %fusion.41), kind=kLoop, calls=%fused_computation.9 | loop fusion | flops 786432 | bytes 3932160 | tf_op jit(solution)/shard_map/convert.3
  415.9 2.9 reshape.382
  418.9 1.5 reshape.383
  422.5 288.6 %all-reduce.2.cloned.1.call-done = bf16[48,2,4,1024]{3,0,2,1:T(8,128)(2,1)} async-done(((bf16[48,2,4,1024]{3,0,2,1:T(8,128)(2,1)}), bf16[48,2,4,1024]{3,0,2,1:T(8,128)(2,1)}) %all-reduce.2.cloned.1.call-update) | async-done | bytes 786448 | tf_op jit(solution)/shard_map/psum | solution.py:110
  711.1 2.9 copy.269
  714.0 1.5 copy.263
  715.6 2.1 fusion.5
  (46 shorter events, 16.0 us)
Async XLA Ops:
  7.2 12.2 %copy-start = (bf16[1,6,768,128]{3,2,1,0:T(8,128)(2,1)S(1)}, bf16[1,6,768,128]{3,2,1,0:T(8,128)(2,1)}, u32[]{:S(2)}) copy-start(bf16[1,6,768,128]{3,2,1,0:T(8,128)(2,1)} %param.5) | copy-start | bytes 3538948
  50.7 21.2 %all-to-all-start.1 = ((bf16[1,48,96,128]{3,1,0,2:T(8,128)(2,1)}), bf16[1,48,96,128]{3,1,0,2:T(8,128)(2,1)S(1)}, u32[]{:S(2)}, u32[]{:S(2)}) async-start(bf16[1,48,96,128]{3,1,0,2:T(8,128)(2,1)} %copy.226), calls=%async_computation.1 | async-start | bytes 2359296 | tf_op jit(solution)/shard_map/all_to_all | solution.py:62
  85.5 4.5 copy-start.3
  85.5 29.0 %all-to-all-start.2 = ((bf16[1,384,12,128]{3,2,0,1:T(8,128)(2,1)}), bf16[1,384,12,128]{3,2,0,1:T(8,128)(2,1)}, u32[]{:S(2)}, u32[]{:S(2)}) async-start(bf16[1,384,12,128]{3,2,0,1:T(8,128)(2,1)} %copy.229), calls=%async_computation.2 | async-start | bytes 3145728 | tf_op jit(solution)/shard_map/all_to_all | solution.py:74
  202.2 25.8 %all-to-all-start.5 = ((bf16[1,48,96,128]{3,2,0,1:T(8,128)(2,1)}), bf16[1,48,96,128]{3,2,0,1:T(8,128)(2,1)}, u32[]{:S(2)}, u32[]{:S(2)}) async-start(bf16[1,48,96,128]{3,2,0,1:T(8,128)(2,1)} %copy.241), calls=%async_computation.5 | async-start | bytes 2359296 | tf_op jit(solution)/shard_map/all_to_all | solution.py:83
  291.5 22.5 %all-to-all-start.8 = ((bf16[1,384,12,128]{3,2,0,1:T(8,128)(2,1)}), bf16[1,384,12,128]{3,2,0,1:T(8,128)(2,1)S(1)}, u32[]{:S(2)}, u32[]{:S(2)}) async-start(bf16[1,384,12,128]{3,2,0,1:T(8,128)(2,1)} %copy.250), calls=%async_computation.8 | async-start | bytes 3145728 | tf_op jit(solution)/shard_map/all_to_all | solution.py:74
  375.5 24.5 %all-to-all-start.10 = ((bf16[1,384,12,128]{3,2,0,1:T(8,128)(2,1)}), bf16[1,384,12,128]{3,2,0,1:T(8,128)(2,1)S(1)}, u32[]{:S(2)}, u32[]{:S(2)}) async-start(bf16[1,384,12,128]{3,2,0,1:T(8,128)(2,1)} %copy.259), calls=%async_computation.10 | async-start | bytes 3145728 | tf_op jit(solution)/shard_map/all_to_all | solution.py:84
  401.8 312.2 %all-to-all-start.11 = ((bf16[1,48,96,128]{3,2,0,1:T(8,128)(2,1)}), bf16[1,48,96,128]{3,2,0,1:T(8,128)(2,1)}, u32[]{:S(2)}, u32[]{:S(2)}) async-start(bf16[1,48,96,128]{3,2,0,1:T(8,128)(2,1)} %copy.262), calls=%async_computation.11 | async-start | bytes 2359296 | tf_op jit(solution)/shard_map/all_to_all | solution.py:83
  408.4 302.7 %all-reduce.2.cloned.1.call-start = ((), (), s32[]{:S(2)}) async-start(), calls=%async_computation.12 | async-start | bytes 1572864 | tf_op jit(solution)/shard_map/psum | solution.py:110
  420.4 1.6 copy-start.2
  714.0 1.6 copy-start.4
  715.6 2.1 copy-start.1
Sparse Core Ops, SparseCore 0:
  421.7 289.3 all-reduce.1
where the time goes:
time: 735 us; the launch traced here: 725 us
  waiting for transfers between devices  325 us (44%)
  local copies, waits for them, and re-layouts  155 us (21%)
  blocking collectives  129 us (18%)
  matrix products  47 us (6%)
  starting transfers between devices  33.3 us (5%)
  other arithmetic  20.7 us (3%)
  between operations  14.5 us (2%)
    psum x1, waiting for transfers between devices, shards(): lax.psum(local_grad.astype(jnp.bfloat16), ('lon', 'dp')).astype(jnp.float32)  289 us
    another operation x11, local copies, waits for them, and re-layouts  55.7 us
    all_to_all x2, blocking collectives, analyze(): lax.all_to_all(spectra, 'lon', split_axis=2, concat_axis=1, tiled=True)  50.5 us
    all_to_all x2, blocking collectives, synthesize(): lax.all_to_all(spectral, 'lat', split_axis=2, concat_axis=1, tiled=True)  39.5 us
    another operation x2, local copies, waits for them, and re-layouts, build_kernel(): return jnp.stack([upper_rows, lower_rows], axis=2)  24.3 us
    all_to_all x1, blocking collectives, synthesize(): lax.all_to_all(spectra, 'lat', split_axis=1, concat_axis=2, tiled=True)  20.7 us
    all_to_all x1, blocking collectives, analyze(): lax.all_to_all(lax.all_to_all(spectra, 'lon', split_axis=2, concat_axis=1...  18.7 us
    all_to_all x2, starting transfers between devices, synthesize(): lax.all_to_all(lax.all_to_all(spectra, 'lat', split_axis=1, concat_axis=2...  15.8 us
  transfers between devices with their start and end apart: 7, of which 4 were waited for; matrix products, arithmetic and copies ran while one was open for 11% of the time, Pallas kernels for 0%

commit v1 on v0

--- a/solution.py
+++ b/solution.py
@@ -35,6 +35,18 @@
     normal_cdf = 0.5 * (1.0 + lax.erf(branch * (1.0 / math.sqrt(2.0))))
     density = jnp.exp(-0.5 * branch * branch) * (1.0 / math.sqrt(2.0 * math.pi))
     return normal_cdf + branch * density
+
+
+def reduce_over(values, axes):
+    count = 1
+    for name in axes:
+        count *= lax.axis_size(name)
+    chunks = values.reshape(count, -1)
+    scattered = lax.all_to_all(chunks, axes, split_axis=0, concat_axis=0, tiled=True)
+    reduced = jnp.sum(scattered.astype(jnp.float32), axis=0).astype(values.dtype)
+    tiled = jnp.broadcast_to(reduced[None], (count, reduced.shape[0]))
+    gathered = lax.all_to_all(tiled, axes, split_axis=0, concat_axis=0, tiled=True)
+    return gathered.reshape(values.shape)
 
 
 def shards(state_grid, cotangent, legendre, wave_ids, weights):
@@ -107,7 +119,7 @@
     real_grad = outer_sums[:, :, 0, :, 0, :] + outer_sums[:, :, 1, :, 1, :]
     imag_grad = outer_sums[:, :, 0, :, 1, :] - outer_sums[:, :, 1, :, 0, :]
     local_grad = jnp.stack([real_grad, imag_grad], axis=1).reshape(weights.shape)
-    weight_grad = lax.psum(local_grad.astype(jnp.bfloat16), ("lon", "dp")).astype(jnp.float32)
+    weight_grad = reduce_over(local_grad.astype(jnp.bfloat16), ("lon", "dp")).astype(jnp.float32)
     demixed = jnp.einsum(
         "slmqgo,lgpiqo->slmpgi", back_six, kernel, preferred_element_type=jnp.float32
     ).astype(jnp.bfloat16)

time: 735 us -> 501 us (0.68)
  waiting for transfers between devices: 325 us -> 80.8 us
  starting transfers between devices: 33.3 us -> 58.2 us
  blocking collectives: 129 us -> 109 us
  between operations: 14.5 us -> 1.51 us
  other arithmetic: 20.7 us -> 33.2 us
  local copies, waits for them, and re-layouts: 155 us -> 166 us
    psum x1 -> x0, waiting for transfers between devices: 289 us -> none  [shards(): lax.psum(local_grad.astype(jnp.bfloat16), ('lon', 'dp')).astype(jnp.float32)]
    all_to_all x0 -> x3, waiting for transfers between devices: none -> 29.3 us  [the longest x1 20.1 us: reduce_over(): lax.all_to_all(tiled, axes, split_axis=0, concat_axis=0, tiled=True)]
    all_to_all x0 -> x3, starting transfers between devices: none -> 22.3 us  [the longest x1 10.7 us: reduce_over(): lax.all_to_all(chunks, axes, split_axis=0, concat_axis=0, tiled=True)]
    all_to_all x2 -> x1, blocking collectives: 39.5 us -> 19.3 us  [synthesize(): lax.all_to_all(spectral, 'lat', split_axis=2, concat_axis=1, tiled=True)]
    convert_element_type x0 -> x2, other arithmetic: none -> 11.2 us  [the longest x1 5.7 us: shards(): reduce_over(local_grad.astype(jnp.bfloat16), ('lon', 'dp'))]
    all_to_all x1, waiting for transfers between devices: 0.01 us -> 9.89 us  [synthesize(): lax.all_to_all(spectra, 'lat', split_axis=1, concat_axis=2, tiled=True)]
    another operation x11 -> x12, local copies, waits for them, and re-layouts: 55.7 us -> 56.2 us
  transfers between devices with their start and end apart: 7 -> 9, of which waited for: 4 -> 7; matrix products, arithmetic and copies ran while one was open for 11% -> 22% of each run, Pallas kernels for 0% -> 0%
where the time goes in v1:
time: 501 us; the launch traced here: 491 us
  local copies, waits for them, and re-layouts  166 us (33%)
  blocking collectives  109 us (22%)
  waiting for transfers between devices  80.8 us (16%)
  starting transfers between devices  58.2 us (12%)
  matrix products  42.3 us (8%)
  other arithmetic  33.2 us (7%)
    another operation x11, local copies, waits for them, and re-layouts  55.6 us
    all_to_all x2, blocking collectives, analyze(): lax.all_to_all(spectra, 'lon', split_axis=2, concat_axis=1, tiled=True)  50.5 us
    another operation x2, local copies, waits for them, and re-layouts, build_kernel(): return jnp.stack([upper_rows, lower_rows], axis=2)  24.3 us
    all_to_all x1, blocking collectives, synthesize(): lax.all_to_all(spectra, 'lat', split_axis=1, concat_axis=2, tiled=True)  20.7 us
    all_to_all x1, waiting for transfers between devices, reduce_over(): lax.all_to_all(tiled, axes, split_axis=0, concat_axis=0, tiled=True)  20.1 us
    all_to_all x2, waiting for transfers between devices, synthesize(): lax.all_to_all(lax.all_to_all(spectra, 'lat', split_axis=1, concat_axis=2...  19.8 us
    all_to_all x1, blocking collectives, synthesize(): lax.all_to_all(spectral, 'lat', split_axis=2, concat_axis=1, tiled=True)  19.3 us
    all_to_all x1, blocking collectives, analyze(): lax.all_to_all(lax.all_to_all(spectra, 'lon', split_axis=2, concat_axis=1...  18.5 us
  transfers between devices with their start and end apart: 9, of which 7 were waited for; matrix products, arithmetic and copies ran while one was open for 22% of the time, Pallas kernels for 0%

profile of v1, /device:TPU:1, one launch (start us, length us, event | category | flops | bytes accessed | tf_op | source)
XLA Modules:
  0.0 491.0 jit_solution(6807148011307107200)
XLA Ops:
  1.7 4.9 %cosine_multiply_fusion = (f32[384,1,768]{2,0,1:T(8,128)S(1)}, f32[384,1,768]{2,0,1:T(8,128)S(1)}) fusion(s32[384]{0:T(512)S(1)} %mul.121), kind=kLoop, calls=%fused_computation.45 | loop fusion | flops 3538944 | bytes 2360832 | tf_op jit(solution)/shard_map/mul | solution.py:18
  6.8 2.2 copy.216
  9.0 3.7 reshape.392
  12.8 2.4 fusion.14
  16.0 26.4 %all_to_all.204 = bf16[1,6,768,128]{3,1,0,2:T(8,128)(2,1)S(1)} all-to-all(bf16[1,6,768,128]{3,1,0,2:T(8,128)(2,1)S(1)} %copy.224), channel_id=1, replica_groups=mesh['lat'=8,'lon'=8,'dp'=4] {'lon'}, dimensions={2} | all-to-all | bytes 2359296 | tf_op jit(solution)/shard_map/all_to_all | solution.py:75
  44.1 6.0 %all-to-all-start.1 = ((bf16[1,48,96,128]{3,1,0,2:T(8,128)(2,1)}), bf16[1,48,96,128]{3,1,0,2:T(8,128)(2,1)S(1)}, u32[]{:S(2)}, u32[]{:S(2)}) async-start(bf16[1,48,96,128]{3,1,0,2:T(8,128)(2,1)} %copy.227), calls=%async_computation.1 | async-start | bytes 2359296 | tf_op jit(solution)/shard_map/all_to_all | solution.py:74
  50.9 14.6 %all-to-all-done.1 = bf16[1,48,96,128]{3,1,0,2:T(8,128)(2,1)S(1)} async-done(((bf16[1,48,96,128]{3,1,0,2:T(8,128)(2,1)}), bf16[1,48,96,128]{3,1,0,2:T(8,128)(2,1)S(1)}, u32[]{:S(2)}, u32[]{:S(2)}) %all-to-all-start.1) | async-done | bytes 1179680 | tf_op jit(solution)/shard_map/all_to_all | solution.py:74
  65.6 3.0 copy.282
  68.5 4.4 reshape.404
  73.0 3.4 convolution_convert_fusion.1
  76.4 2.9 copy.230
  79.3 4.5 all-to-all-start.2
  87.7 2.2 copy.301
  90.0 2.7 maximum_bitcast_fusion
  92.7 3.0 pad_maximum_fusion
  95.6 12.7 %copy.233 = bf16[48,4,2,32,2,32]{3,5,2,4,1,0:T(8,128)(2,1)} copy(bf16[48,4,2,32,2,32]{0,5,4,3,1,2:T(8,128)(2,1)} %pad_maximum_fusion) | data formatting | bytes 3145728 | tf_op jit(solution)/shard_map/stack | solution.py:31
  110.1 2.8 copy.232
  112.9 8.3 %copy.272 = bf16[48,48,2,4,32,1]{1,4,2,5,3,0:T(8,128)(2,1)} copy(bf16[48,48,2,4,32,1]{0,4,3,2,1,5:T(8,128)(2,1)} %bitcast.179) | data formatting | bytes 2359296 | tf_op jit(solution)/shard_map/reshape.8
  121.2 6.7 %fusion = bf16[1,48,48,2,4,32]{2,5,3,4,1,0:T(8,128)(2,1)} fusion(bf16[48,4,2,32,2,32]{3,5,2,4,1,0:T(8,128)(2,1)} %copy.233, bf16[48,48,2,4,32,1]{1,4,2,5,3,0:T(8,128)(2,1)} %copy.272), kind=kOutput, calls=%fused_computation.4 | convolution fusion | flops 76087296 | bytes 3932160 | tf_op jit(solution)/shard_map/slmpgi,lgpiqo->slmqgo/dot_general | solution.py:109
  127.9 8.3 %copy.235 = bf16[1,48,48,2,4,32]{1,5,4,3,2,0:T(8,128)(2,1)} copy(bf16[1,48,48,2,4,32]{2,5,3,4,1,0:T(8,128)(2,1)} %fusion) | data formatting | bytes 2359296 | tf_op jit(solution)/shard_map/convert_element_type | solution.py:111
  136.1 3.2 copy.236
  139.3 19.3 %all_to_all.205 = bf16[1,48,96,128]{3,1,0,2:T(8,128)(2,1)} all-to-all(bf16[1,48,96,128]{3,1,0,2:T(8,128)(2,1)S(1)} %copy.236), channel_id=1, replica_groups=mesh['lat'=8,'lon'=8,'dp'=4] {'lat'}, dimensions={2} | all-to-all | bytes 2359296 | tf_op jit(solution)/shard_map/all_to_all | solution.py:89
  158.6 4.2 copy.285
  162.8 4.4 reshape.405
  167.2 3.5 convolution_convert_fusion.3
  170.7 2.9 copy.239
  173.6 20.7 %all_to_all.206 = bf16[1,384,12,128]{3,2,0,1:T(8,128)(2,1)S(1)} all-to-all(bf16[1,384,12,128]{3,2,0,1:T(8,128)(2,1)} %copy.239), channel_id=1, replica_groups=mesh['lat'=8,'lon'=8,'dp'=4] {'lat'}, dimensions={1} | all-to-all | bytes 2359296 | tf_op jit(solution)/shard_map/all_to_all | solution.py:96
  196.1 9.2 %all-to-all-start.5 = ((bf16[1,48,96,128]{3,2,0,1:T(8,128)(2,1)}), bf16[1,48,96,128]{3,2,0,1:T(8,128)(2,1)}, u32[]{:S(2)}, u32[]{:S(2)}) async-start(bf16[1,48,96,128]{3,2,0,1:T(8,128)(2,1)} %copy.242), calls=%async_computation.5 | async-start | bytes 2359296 | tf_op jit(solution)/shard_map/all_to_all | solution.py:95
  207.6 14.2 %all-to-all-done.5 = bf16[1,48,96,128]{3,2,0,1:T(8,128)(2,1)} async-done(((bf16[1,48,96,128]{3,2,0,1:T(8,128)(2,1)}), bf16[1,48,96,128]{3,2,0,1:T(8,128)(2,1)}, u32[]{:S(2)}, u32[]{:S(2)}) %all-to-all-start.5) | async-done | bytes 1179680 | tf_op jit(solution)/shard_map/all_to_all | solution.py:95
  223.2 4.8 fusion.15
  230.1 24.1 %all_to_all.207 = bf16[1,6,768,128]{3,1,0,2:T(8,128)(2,1)S(1)} all-to-all(bf16[1,6,768,128]{3,1,0,2:T(8,128)(2,1)S(1)} %copy.245), channel_id=1, replica_groups=mesh['lat'=8,'lon'=8,'dp'=4] {'lon'}, dimensions={2} | all-to-all | bytes 2359296 | tf_op jit(solution)/shard_map/all_to_all | solution.py:75
  254.9 18.5 %all_to_all.208 = bf16[1,48,96,128]{3,1,0,2:T(8,128)(2,1)S(1)} all-to-all(bf16[1,48,96,128]{3,1,0,2:T(8,128)(2,1)S(1)} %copy.248), channel_id=1, replica_groups=mesh['lat'=8,'lon'=8,'dp'=4] {'lat'}, dimensions={2} | all-to-all | bytes 2359296 | tf_op jit(solution)/shard_map/all_to_all | solution.py:74
  273.4 3.0 copy.286
  276.4 4.4 reshape.406
  280.8 2.4 convolution_convert_fusion
  285.1 3.6 all-to-all-start.8
  288.7 11.6 %copy.254 = bf16[48,4,2,32,2,32]{5,3,4,2,1,0:T(8,128)(2,1)} copy(bf16[48,4,2,32,2,32]{0,5,4,3,1,2:T(8,128)(2,1)} %pad_maximum_fusion) | data formatting | bytes 3145728 | tf_op jit(solution)/shard_map/stack | solution.py:31
  300.3 7.3 %all-to-all-done.8 = bf16[1,384,12,128]{3,2,0,1:T(8,128)(2,1)S(1)} async-done(((bf16[1,384,12,128]{3,2,0,1:T(8,128)(2,1)}), bf16[1,384,12,128]{3,2,0,1:T(8,128)(2,1)S(1)}, u32[]{:S(2)}, u32[]{:S(2)}) %all-to-all-start.8) | async-done | bytes 1179680 | tf_op jit(solution)/shard_map/all_to_all | solution.py:86
  307.9 2.8 copy.253
  310.7 8.3 %copy.275 = bf16[48,48,2,4,32,1]{1,4,2,5,3,0:T(8,128)(2,1)} copy(bf16[48,48,2,4,32,1]{0,4,3,2,1,5:T(8,128)(2,1)} %bitcast.182) | data formatting | bytes 2359296 | tf_op jit(solution)/shard_map/reshape.41
  318.9 6.7 %fusion.1 = bf16[1,48,48,2,4,32]{2,5,3,4,1,0:T(8,128)(2,1)} fusion(bf16[48,4,2,32,2,32]{5,3,4,2,1,0:T(8,128)(2,1)} %copy.254, bf16[48,48,2,4,32,1]{1,4,2,5,3,0:T(8,128)(2,1)} %copy.275), kind=kOutput, calls=%fused_computation.5 | convolution fusion | flops 76087296 | bytes 3932160 | tf_op jit(solution)/shard_map/slmqgo,lgpiqo->slmpgi/dot_general | solution.py:123
  325.7 8.3 %copy.256 = bf16[1,48,48,2,4,32]{1,5,4,3,2,0:T(8,128)(2,1)} copy(bf16[1,48,48,2,4,32]{2,5,3,4,1,0:T(8,128)(2,1)} %fusion.1) | data formatting | bytes 2359296 | tf_op jit(solution)/shard_map/convert_element_type | solution.py:125
  333.9 4.1 copy.257
  338.1 5.1 %all-to-all-start.9 = ((bf16[1,48,96,128]{3,1,0,2:T(8,128)(2,1)}), bf16[1,48,96,128]{3,1,0,2:T(8,128)(2,1)S(1)}, u32[]{:S(2)}, u32[]{:S(2)}) async-start(bf16[1,48,96,128]{3,1,0,2:T(8,128)(2,1)} %copy.257), calls=%async_computation.9 | async-start | bytes 2359296 | tf_op jit(solution)/shard_map/all_to_all | solution.py:89
  343.1 8.3 %copy.278 = bf16[48,48,2,4,32,1]{1,4,5,2,3,0:T(8,128)(2,1)} copy(bf16[48,48,2,4,32,1]{0,4,3,2,1,5:T(8,128)(2,1)} %bitcast.180) | data formatting | bytes 2359296 | tf_op jit(solution)/shard_map/reshape.8
  351.4 8.0 %fusion.41 = f32[48,4,2,32,2,32]{5,3,4,2,1,0:T(8,128)S(1)} fusion(bf16[48,48,2,4,32,1]{1,4,5,2,3,0:T(8,128)(2,1)} %copy.278, bf16[48,48,2,4,32,1]{1,4,2,5,3,0:T(8,128)(2,1)} %copy.275), kind=kOutput, calls=%fused_computation.67 | convolution fusion | flops 75497472 | bytes 5505024 | tf_op jit(solution)/shard_map/slmpgi,slmqgo->lgpiqo/dot_general | solution.py:116
  359.4 2.7 fusion.3
  362.1 2.9 reshape.408
  368.9 5.5 %reduce.4 = bf16[32,12288]{1,0:T(8,128)(2,1)S(1)} reduce(bf16[32,1,12288]{2,1,0:T(2,128)(2,1)S(1)} %convert_element_type.184, bf16[]{:T(256)} %broadcast.163), dimensions={1}, to_apply=%convert_element_type.184.reduce_sub_computation | reduce | bytes 1572866 | tf_op jit(solution)/shard_map/convert_element_type | solution.py:122
  375.8 10.7 %all-to-all-start.12 = ((bf16[32,2,6144]{2,1,0:T(2,128)(2,1)}), bf16[32,2,6144]{2,1,0:T(2,128)(2,1)S(1)}, u32[]{:S(2)}, u32[]{:S(2)}) async-start(bf16[32,2,6144]{2,1,0:T(2,128)(2,1)} %reshape.413), calls=%async_computation.12 | async-start | bytes 1572864 | tf_op jit(solution)/shard_map/all_to_all | solution.py:45
  386.5 3.0 copy.289
  389.4 4.4 reshape.407
  393.9 2.4 convolution_convert_fusion.2
  398.3 9.2 %all-to-all-done.12 = bf16[32,2,6144]{2,1,0:T(2,128)(2,1)S(1)} async-done(((bf16[32,2,6144]{2,1,0:T(2,128)(2,1)}), bf16[32,2,6144]{2,1,0:T(2,128)(2,1)S(1)}, u32[]{:S(2)}, u32[]{:S(2)}) %all-to-all-start.12) | async-done | bytes 786464 | tf_op jit(solution)/shard_map/all_to_all | solution.py:45
  407.5 8.1 %all-to-all-start.10 = ((bf16[1,384,12,128]{3,2,0,1:T(8,128)(2,1)}), bf16[1,384,12,128]{3,2,0,1:T(8,128)(2,1)}, u32[]{:S(2)}, u32[]{:S(2)}) async-start(bf16[1,384,12,128]{3,2,0,1:T(8,128)(2,1)} %copy.260), calls=%async_computation.10 | async-start | bytes 3145728 | tf_op jit(solution)/shard_map/all_to_all | solution.py:96
  419.3 5.5 %reduce.5 = bf16[32,12288]{1,0:T(8,128)(2,1)S(1)} reduce(bf16[32,1,12288]{2,1,0:T(2,128)(2,1)S(1)} %broadcast_in_dim.34, bf16[]{:T(256)} %broadcast.163), dimensions={1}, to_apply=%broadcast_in_dim.34.reduce_sub_computation | reduce | bytes 1572866 | tf_op jit(solution)/shard_map/broadcast_in_dim | solution.py:47
  426.3 9.9 %all-to-all-done.10 = bf16[1,384,12,128]{3,2,0,1:T(8,128)(2,1)} async-done(((bf16[1,384,12,128]{3,2,0,1:T(8,128)(2,1)}), bf16[1,384,12,128]{3,2,0,1:T(8,128)(2,1)}, u32[]{:S(2)}, u32[]{:S(2)}) %all-to-all-start.10) | async-done | bytes 1179680 | tf_op jit(solution)/shard_map/all_to_all | solution.py:96
  436.2 6.6 %all-to-all-start.13 = ((bf16[32,2,6144]{2,1,0:T(2,128)(2,1)}), bf16[32,2,6144]{2,1,0:T(2,128)(2,1)S(1)}, u32[]{:S(2)}, u32[]{:S(2)}) async-start(bf16[32,2,6144]{2,1,0:T(2,128)(2,1)} %reshape.415), calls=%async_computation.13 | async-start | bytes 1572864 | tf_op jit(solution)/shard_map/all_to_all | solution.py:48
  445.9 20.1 %all-to-all-done.13 = bf16[32,2,6144]{2,1,0:T(2,128)(2,1)S(1)} async-done(((bf16[32,2,6144]{2,1,0:T(2,128)(2,1)}), bf16[32,2,6144]{2,1,0:T(2,128)(2,1)S(1)}, u32[]{:S(2)}, u32[]{:S(2)}) %all-to-all-start.13) | async-done | bytes 786464 | tf_op jit(solution)/shard_map/all_to_all | solution.py:48
  466.0 4.5 all-to-all-start.11
  472.5 5.7 %convert_reduce_fusion = f32[32,12288]{1,0:T(8,128)} fusion(bf16[32,1,12288]{2,1,0:T(2,128)(2,1)S(1)} %reshape.416), kind=kLoop, calls=%fused_computation.29 | loop fusion | flops 393216 | bytes 2359296 | tf_op jit(solution)/shard_map/convert_element_type | solution.py:122
  478.2 3.2 reshape.391
  481.5 5.6 %all-to-all-done.11 = bf16[1,48,96,128]{3,2,0,1:T(8,128)(2,1)} async-done(((bf16[1,48,96,128]{3,2,0,1:T(8,128)(2,1)}), bf16[1,48,96,128]{3,2,0,1:T(8,128)(2,1)}, u32[]{:S(2)}, u32[]{:S(2)}) %all-to-all-start.11) | async-done | bytes 1179680 | tf_op jit(solution)/shard_map/all_to_all | solution.py:95
  488.4 2.1 fusion.5
  (62 shorter events, 39.8 us)
Async XLA Ops:
  0.6 12.2 %copy-start = (bf16[1,6,768,128]{3,2,1,0:T(8,128)(2,1)S(1)}, bf16[1,6,768,128]{3,2,1,0:T(8,128)(2,1)}, u32[]{:S(2)}) copy-start(bf16[1,6,768,128]{3,2,1,0:T(8,128)(2,1)} %param.5) | copy-start | bytes 3538948
  44.1 21.4 %all-to-all-start.1 = ((bf16[1,48,96,128]{3,1,0,2:T(8,128)(2,1)}), bf16[1,48,96,128]{3,1,0,2:T(8,128)(2,1)S(1)}, u32[]{:S(2)}, u32[]{:S(2)}) async-start(bf16[1,48,96,128]{3,1,0,2:T(8,128)(2,1)} %copy.227), calls=%async_computation.1 | async-start | bytes 2359296 | tf_op jit(solution)/shard_map/all_to_all | solution.py:74
  79.3 4.5 copy-start.4
  79.3 29.1 %all-to-all-start.2 = ((bf16[1,384,12,128]{3,2,0,1:T(8,128)(2,1)}), bf16[1,384,12,128]{3,2,0,1:T(8,128)(2,1)}, u32[]{:S(2)}, u32[]{:S(2)}) async-start(bf16[1,384,12,128]{3,2,0,1:T(8,128)(2,1)} %copy.230), calls=%async_computation.2 | async-start | bytes 3145728 | tf_op jit(solution)/shard_map/all_to_all | solution.py:86
  196.1 25.8 %all-to-all-start.5 = ((bf16[1,48,96,128]{3,2,0,1:T(8,128)(2,1)}), bf16[1,48,96,128]{3,2,0,1:T(8,128)(2,1)}, u32[]{:S(2)}, u32[]{:S(2)}) async-start(bf16[1,48,96,128]{3,2,0,1:T(8,128)(2,1)} %copy.242), calls=%async_computation.5 | async-start | bytes 2359296 | tf_op jit(solution)/shard_map/all_to_all | solution.py:95
  285.1 22.5 %all-to-all-start.8 = ((bf16[1,384,12,128]{3,2,0,1:T(8,128)(2,1)}), bf16[1,384,12,128]{3,2,0,1:T(8,128)(2,1)S(1)}, u32[]{:S(2)}, u32[]{:S(2)}) async-start(bf16[1,384,12,128]{3,2,0,1:T(8,128)(2,1)} %copy.251), calls=%async_computation.8 | async-start | bytes 3145728 | tf_op jit(solution)/shard_map/all_to_all | solution.py:86
  338.1 37.7 %all-to-all-start.9 = ((bf16[1,48,96,128]{3,1,0,2:T(8,128)(2,1)}), bf16[1,48,96,128]{3,1,0,2:T(8,128)(2,1)S(1)}, u32[]{:S(2)}, u32[]{:S(2)}) async-start(bf16[1,48,96,128]{3,1,0,2:T(8,128)(2,1)} %copy.257), calls=%async_computation.9 | async-start | bytes 2359296 | tf_op jit(solution)/shard_map/all_to_all | solution.py:89
  375.8 31.7 %all-to-all-start.12 = ((bf16[32,2,6144]{2,1,0:T(2,128)(2,1)}), bf16[32,2,6144]{2,1,0:T(2,128)(2,1)S(1)}, u32[]{:S(2)}, u32[]{:S(2)}) async-start(bf16[32,2,6144]{2,1,0:T(2,128)(2,1)} %reshape.413), calls=%async_computation.12 | async-start | bytes 1572864 | tf_op jit(solution)/shard_map/all_to_all | solution.py:45
  407.5 28.7 %all-to-all-start.10 = ((bf16[1,384,12,128]{3,2,0,1:T(8,128)(2,1)}), bf16[1,384,12,128]{3,2,0,1:T(8,128)(2,1)}, u32[]{:S(2)}, u32[]{:S(2)}) async-start(bf16[1,384,12,128]{3,2,0,1:T(8,128)(2,1)} %copy.260), calls=%async_computation.10 | async-start | bytes 3145728 | tf_op jit(solution)/shard_map/all_to_all | solution.py:96
  436.2 29.8 %all-to-all-start.13 = ((bf16[32,2,6144]{2,1,0:T(2,128)(2,1)}), bf16[32,2,6144]{2,1,0:T(2,128)(2,1)S(1)}, u32[]{:S(2)}, u32[]{:S(2)}) async-start(bf16[32,2,6144]{2,1,0:T(2,128)(2,1)} %reshape.415), calls=%async_computation.13 | async-start | bytes 1572864 | tf_op jit(solution)/shard_map/all_to_all | solution.py:48
  445.9 24.6 %copy-start.2 = (bf16[384,2,768]{2,1,0:T(2,128)(2,1)S(1)}, bf16[384,2,768]{2,1,0:T(2,128)(2,1)}, u32[]{:S(2)}) copy-start(bf16[384,2,768]{2,1,0:T(2,128)(2,1)} %copy.216) | copy-start | bytes 3538948
  466.0 21.1 %all-to-all-start.11 = ((bf16[1,48,96,128]{3,2,0,1:T(8,128)(2,1)}), bf16[1,48,96,128]{3,2,0,1:T(8,128)(2,1)}, u32[]{:S(2)}, u32[]{:S(2)}) async-start(bf16[1,48,96,128]{3,2,0,1:T(8,128)(2,1)} %copy.263), calls=%async_computation.11 | async-start | bytes 2359296 | tf_op jit(solution)/shard_map/all_to_all | solution.py:95
  481.5 6.9 %copy-start.3 = (bf16[768,768]{1,0:T(8,128)(2,1)S(1)}, bf16[768,768]{1,0:T(8,128)(2,1)}, u32[]{:S(2)}) copy-start(bf16[768,768]{1,0:T(8,128)(2,1)} %convert_element_type.151) | copy-start | bytes 3538948
  481.5 7.0 %copy-start.5 = (bf16[1,6,768,128]{3,2,1,0:T(8,128)(2,1)S(1)}, bf16[1,6,768,128]{3,2,1,0:T(8,128)(2,1)}, u32[]{:S(2)}) copy-start(bf16[1,6,768,128]{3,2,1,0:T(8,128)(2,1)} %param.6) | copy-start | bytes 3538948
  488.4 2.2 copy-start.1
